TPU v7x, 512 devices: a whole 4x8x8 slice. The times are simulated.
512 devices in a mesh: grp: 16 (over z, core), dev: 32 (over x, y).
Axes of the slice: x: 4, y: 8, z: 8, core: 2. Of those that a mesh axis runs over, the one named last changes fastest.
Arguments:
- ssm_input: bfloat16 [4096, 4096], P('grp', 'dev'), may hold values from -6 to 6
- gate_input: bfloat16 [4096, 4096], P('grp', 'dev'), may hold values from -6 to 6
- step_size: float32 [4096, 64], P('grp', 'dev'), may hold values from 6.1035156e-05 to 0.3375
- decay_rate: float32 [64], P('dev'), may hold values from 0.5 to 2
- in_coeff: bfloat16 [4096, 128], P('grp'), may hold values from -6 to 6
- out_coeff: bfloat16 [4096, 128], P('grp'), may hold values from -6 to 6
- skip_gain: float32 [64], P('dev'), may hold values from 0.5 to 3
- norm_gain: float32 [4096], P('dev'), may hold values from 0.5 to 1.5
- out_proj: bfloat16 [4096, 2048], P(None, 'dev'), may hold values from -0.09375 to 0.09375
- residual: bfloat16 [4096, 2048], P(('grp', 'dev')), may hold values from -6 to 6
- ffn_gain: float32 [2048], replicated, may hold values from 0.5 to 1.5
- router: float32 [2048, 16], replicated, may hold values from -0.125 to 0.125
- routes: int32 [4096, 2], P(('grp', 'dev')), may hold values from 0 to 15, all different within a row; in each aligned block of 8 rows (0 to 7, 8 to 15, ...) at most 2 rows name the same one
- gate_weight: bfloat16 [16, 2048, 8192], P('grp', None, 'dev'), may hold values from -0.125 to 0.125
- up_weight: bfloat16 [16, 2048, 8192], P('grp', None, 'dev'), may hold values from -0.125 to 0.125
- down_weight: bfloat16 [16, 8192, 2048], P('grp', 'dev'), may hold values from -0.0625 to 0.0625
Outputs:
- moe_out: bfloat16 [4096, 2048], P(('grp', 'dev'))
Inputs may be any that keep to these rules, and one draw needn't show every extreme that they name: `routes`: each row names two different experts; among the 8 rows of one dispatch block of consecutive tokens no expert is named more than 2 times, a bound that some block reaches.
All inputs are finite; a program needn't handle non-finite values.
Results may differ from a plain program's by a relative error of at most 0.012.
Values may be sent and summed in bfloat16 or wider, within the bound.
No kernel may reach another device: no remote copies, remote signals or barrier semaphores. Data moves between devices by JAX's collectives and lax.ppermute only.
A program may use at most 64 MiB of HBM per device.

v0:
```python
import jax
import jax.numpy as jnp
from jax import lax
from jax.sharding import Mesh
from jax.sharding import PartitionSpec as P

DEV = ("dev_0", "dev_1")
GRP_DEV = ("grp", "dev_0", "dev_1")
EPSILON = 1e-05
HIGHEST_PREC = lax.Precision.HIGHEST


def side_by_side(arrays, axis, dim, along):
    columns = [a.reshape(*a.shape[:along], -1) for a in arrays]
    both = jnp.concatenate(columns, axis=along)
    filled, at, finished = (lax.all_gather(both, axis, axis=dim, tiled=True), 0, [])
    for a, column in zip(arrays, columns):
        piece = filled[..., at : at + column.shape[along]]
        finished.append(piece.reshape(*piece.shape[:along], *a.shape[along:]))
        at += column.shape[along]
    return tuple(finished)


def sent_to_all(shard, axis):
    peers = lax.axis_size(axis)
    return lax.all_to_all(
        jnp.broadcast_to(shard[None], (peers, *shard.shape)), axis, 0, 0, tiled=True
    )


def of_everyone(shard, axis):
    everything = sent_to_all(shard, axis)
    return jnp.sum(everything, axis=0)


def in_order(tiles, dim):
    dims = list(tiles.shape[1:])
    dims[dim] *= tiles.shape[0]
    return jnp.moveaxis(tiles, 0, dim).reshape(dims)


def collect(shard, axis, dim):
    return in_order(sent_to_all(shard, axis), dim)


def sum_by_axis(terms, axes):
    total = terms.astype(jnp.bfloat16)
    for axis in axes:
        total = lax.psum_scatter(total, axis, scatter_dimension=0, tiled=True)
    return total.astype(jnp.float32)


def rms_scale(values, gain_vec):
    return (
        values * lax.rsqrt(jnp.mean(values * values, axis=-1, keepdims=True) + EPSILON) * gain_vec
    )


def slot_tables(routes_block, expert_count, slot_cap):
    blocks, row_total = (routes_block.shape[0], routes_block.shape[1])
    flat_routes = routes_block.reshape(blocks, row_total * 2)
    onehot = (
        flat_routes[:, :, None] == jnp.arange(expert_count, dtype=jnp.int32)[None, None, :]
    ).astype(jnp.int32)
    earlier = jnp.cumsum(onehot, axis=1) - onehot
    slot_rank = jnp.sum(earlier * onehot, axis=2)
    slot_index = (flat_routes * slot_cap + slot_rank).reshape(blocks, row_total, 2)
    placed = (
        slot_index[:, :, :, None]
        == jnp.arange(expert_count * slot_cap, dtype=jnp.int32)[None, None, None, :]
    )
    return placed.astype(jnp.float32)


def shards(
    ssm_input,
    gate_input,
    step_size,
    decay_rate,
    in_coeff,
    out_coeff,
    skip_gain,
    norm_gain,
    out_proj,
    residual,
    ffn_gain,
    router,
    routes,
    gate_weight,
    up_weight,
    down_weight,
):
    tok_rows = ssm_input.shape[0]
    head_count = step_size.shape[1]
    head_width = ssm_input.shape[1] // head_count
    dev_count = lax.axis_size(DEV)
    inner_dim = ssm_input.shape[1] * dev_count
    block_rows = residual.shape[0]
    model_dim = residual.shape[1]
    experts = lax.axis_size("grp")
    slot_cap = max(2, 4 * block_rows // experts)
    group_slots = experts * slot_cap
    inputs_f = ssm_input.astype(jnp.float32).reshape(tok_rows, head_count, head_width)
    in_float = in_coeff.astype(jnp.float32)
    out_float = out_coeff.astype(jnp.float32)
    log_rate = -(step_size * decay_rate[None, :])
    cumulative = jnp.cumsum(log_rate, axis=0)
    causal = (jnp.arange(tok_rows)[:, None] >= jnp.arange(tok_rows)[None, :])[:, :, None]
    spread = cumulative[:, None, :] - cumulative[None, :, :]
    decay_pair = jnp.where(causal, jnp.exp(jnp.where(causal, spread, 0.0)), 0.0)
    scores = jnp.dot(out_coeff, in_coeff.T, preferred_element_type=jnp.float32)
    mixing = decay_pair * scores[:, :, None] * step_size[None, :, :]
    inside = jnp.einsum("tuh,uhp->thp", mixing, inputs_f, precision=HIGHEST_PREC)
    to_end = jnp.exp(cumulative[-1][None, :] - cumulative) * step_size
    own_state = jnp.einsum("uh,uhp,un->hpn", to_end, inputs_f, in_float, precision=HIGHEST_PREC)
    own_log = cumulative[-1]
    group_logs, group_states = tuple(
        (
            part.astype(jnp.float32)
            for part in side_by_side(
                (own_log[None].astype(jnp.bfloat16), own_state[None].astype(jnp.bfloat16)),
                "grp",
                0,
                2,
            )
        )
    )
    group_index = jnp.arange(group_logs.shape[0])
    my_group = lax.axis_index("grp")
    inclusive = jnp.cumsum(group_logs, axis=0)
    exclusive = inclusive - group_logs
    before_me = jnp.sum(jnp.where((group_index == my_group)[:, None], exclusive, 0.0), axis=0)
    earlier_mask = (group_index < my_group)[:, None]
    weighting = jnp.where(
        earlier_mask, jnp.exp(jnp.where(earlier_mask, before_me[None, :] - inclusive, 0.0)), 0.0
    )
    entering = jnp.einsum("gh,ghpn->hpn", weighting, group_states, precision=HIGHEST_PREC)
    carried = jnp.exp(cumulative)[:, :, None] * jnp.einsum(
        "hpn,tn->thp", entering, out_float, precision=HIGHEST_PREC
    )
    ssm_out = inside + carried + skip_gain[None, :, None] * inputs_f
    gated_out = ssm_out.reshape(tok_rows, head_count * head_width) * jax.nn.silu(
        gate_input.astype(jnp.float32)
    )
    squares = of_everyone(jnp.sum(gated_out * gated_out, axis=1), DEV)
    mixed_rows = (
        gated_out * lax.rsqrt(squares[:, None] / inner_dim + EPSILON) * norm_gain[None, :]
    ).astype(jnp.bfloat16)
    projected = jnp.dot(
        collect(mixed_rows, DEV, 1), out_proj, preferred_element_type=jnp.float32
    ).astype(jnp.bfloat16)
    mamba_out = lax.all_to_all(projected, DEV, split_axis=0, concat_axis=1, tiled=True)
    hidden_res = (residual.astype(jnp.float32) + mamba_out.astype(jnp.float32)).astype(jnp.bfloat16)
    hidden_float = hidden_res.astype(jnp.float32)
    normed = rms_scale(hidden_float, ffn_gain).astype(jnp.bfloat16)
    logits = jnp.dot(normed.astype(jnp.float32), router, precision=HIGHEST_PREC)
    expert_ids = jnp.arange(experts, dtype=jnp.int32)[None, :]
    first_logit = jnp.sum(logits * (routes[:, 0:1] == expert_ids).astype(jnp.float32), axis=1)
    second_logit = jnp.sum(logits * (routes[:, 1:2] == expert_ids).astype(jnp.float32), axis=1)
    first_prob = jax.nn.sigmoid(first_logit - second_logit)
    second_prob = 1.0 - first_prob
    placed = slot_tables(routes[None], experts, slot_cap)[0]
    filled = jnp.sum(placed, axis=1)
    outgoing = jnp.dot(
        filled.T.astype(jnp.bfloat16), normed, preferred_element_type=jnp.float32
    ).astype(jnp.bfloat16)
    outgoing = outgoing.reshape(experts, slot_cap, model_dim)
    arrived = lax.all_to_all(outgoing, "grp", split_axis=0, concat_axis=0, tiled=True)
    all_rows = lax.all_gather(arrived, DEV, axis=0, tiled=True).reshape(-1, model_dim)
    gate_act = jnp.dot(all_rows, gate_weight[0], preferred_element_type=jnp.float32)
    up_act = jnp.dot(all_rows, up_weight[0], preferred_element_type=jnp.float32)
    hidden = (jax.nn.silu(gate_act) * up_act).astype(jnp.bfloat16)
    summed = sum_by_axis(jnp.dot(hidden, down_weight[0], preferred_element_type=jnp.float32), DEV)
    returned = lax.all_to_all(
        summed.astype(jnp.bfloat16).reshape(experts, slot_cap, model_dim),
        "grp",
        split_axis=0,
        concat_axis=0,
        tiled=True,
    )
    weights = first_prob[:, None] * placed[:, 0, :] + second_prob[:, None] * placed[:, 1, :]
    contrib = jnp.dot(
        weights,
        returned.reshape(group_slots, model_dim).astype(jnp.float32),
        precision=HIGHEST_PREC,
    )
    return (hidden_float + contrib).astype(jnp.bfloat16)


def solution(mesh):
    torus = Mesh(mesh.devices.reshape(mesh.shape["grp"], 4, 8), ("grp", "dev_0", "dev_1"))
    in_specs = (
        P("grp", DEV),
        P("grp", DEV),
        P("grp", DEV),
        P(DEV),
        P("grp", None),
        P("grp", None),
        P(DEV),
        P(DEV),
        P(None, DEV),
        P(GRP_DEV, None),
        P(),
        P(),
        P(GRP_DEV, None),
        P("grp", None, DEV),
        P("grp", None, DEV),
        P("grp", DEV, None),
    )
    out_specs = P(GRP_DEV, None)
    return jax.shard_map(
        shards, mesh=torus, in_specs=in_specs, out_specs=out_specs, check_vma=False
    )
```

profile of v0, /device:TPU:1, one launch (start us, length us, event | category | flops | bytes accessed | tf_op | source)
XLA Modules:
  0.0 366.3 jit_solution(13563389187455256031)
XLA Ops:
  6.6 0.9 negate_bitcast_fusion
  7.4 0.6 reduce-window.6
  8.1 0.2 slice_reduce_fusion
  8.2 0.2 reduce-window.9
  8.4 0.1 add_bitcast_fusion
  8.5 0.2 slice_reduce_fusion.1
  8.7 0.1 fusion.52
  8.7 0.9 copy.73
  9.7 0.8 fusion.55
  10.4 1.0 convolution_convert_fusion.2
  11.5 0.1 pad_maximum_fusion
  11.6 26.0 %all_gather.6 = bf16[16,2,8193]{2,1,0:T(2,128)(2,1)S(1)} all-gather(bf16[1,2,8193]{2,1,0:T(2,128)(2,1)S(1)} %pad_maximum_fusion), channel_id=1, replica_groups=mesh['grp'=16,'dev_0'=4,'dev_1'=8] {'grp'}, dimensions={0}, use_global_device_ids=true | all-gather | bytes 557124 | tf_op jit(solution)/shard_map/all_gather | solution.py:16
  37.6 0.7 slice.40
  38.3 0.1 copy.90
  38.4 0.1 copy.76
  38.5 0.1 select_reduce_fusion.1
  38.6 0.1 select_bitcast_fusion
  38.7 0.1 copy.86
  38.8 0.4 reshape.245
  39.2 1.1 fusion.56
  40.3 0.5 fusion.15
  40.8 0.2 fusion.4
  41.1 0.6 fusion.3
  41.7 0.1 copy.78
  41.8 0.1 multiply_reduce_fusion
  42.0 18.2 %all_to_all.34 = f32[32,1,256]{2,1,0:T(1,128)S(1)} all-to-all(f32[32,1,256]{2,1,0:T(1,128)S(1)} %broadcast_in_dim.80), channel_id=1, replica_groups=mesh['grp'=16,'dev_0'=4,'dev_1'=8] {'dev_0','dev_1'}, dimensions={0} | all-to-all | bytes 65536 | tf_op jit(solution)/shard_map/all_to_all | solution.py:26
  60.2 0.1 reduce_sum.76
  60.3 0.1 multiply_convert_fusion
  60.4 0.1 copy.80
  60.5 1.6 broadcast_in_dim.81
  62.1 4.1 %all-to-all-start.1 = ((bf16[32,256,128]{1,2,0:T(8,128)(2,1)}), bf16[32,256,128]{1,2,0:T(8,128)(2,1)S(1)}, u32[]{:S(2)}, u32[]{:S(2)}) async-start(bf16[32,256,128]{1,2,0:T(8,128)(2,1)} %broadcast_in_dim.81), calls=%async_computation.1 | async-start | bytes 4194304 | tf_op jit(solution)/shard_map/all_to_all | solution.py:26
  66.3 0.1 copy.83
  66.3 0.1 eq.90
  66.4 0.1 fusion.40
  66.5 0.2 select_reduce_fusion
  66.7 0.1 reduce_sum.81
  66.8 0.1 copy.85
  66.9 48.6 %all-to-all-done.1 = bf16[32,256,128]{1,2,0:T(8,128)(2,1)S(1)} async-done(((bf16[32,256,128]{1,2,0:T(8,128)(2,1)}), bf16[32,256,128]{1,2,0:T(8,128)(2,1)S(1)}, u32[]{:S(2)}, u32[]{:S(2)}) %all-to-all-start.1) | async-done | bytes 2097184 | tf_op jit(solution)/shard_map/all_to_all | solution.py:26
  115.5 1.5 convolution_convert_fusion.3
  117.0 0.1 copy.81
  117.1 0.7 reshape.260
  117.9 6.4 %all-to-all-start.2 = ((bf16[32,2,256]{2,1,0:T(2,128)(2,1)}), bf16[32,2,256]{2,1,0:T(2,128)(2,1)S(1)}, u32[]{:S(2)}, u32[]{:S(2)}) async-start(bf16[32,2,256]{2,1,0:T(2,128)(2,1)} %reshape.260), calls=%async_computation.2 | async-start | bytes 65536 | tf_op jit(solution)/shard_map/all_to_all | solution.py:152
  124.3 0.1 fusion.48
  124.4 8.6 %all-to-all-done.2 = bf16[32,2,256]{2,1,0:T(2,128)(2,1)S(1)} async-done(((bf16[32,2,256]{2,1,0:T(2,128)(2,1)}), bf16[32,2,256]{2,1,0:T(2,128)(2,1)S(1)}, u32[]{:S(2)}, u32[]{:S(2)}) %all-to-all-start.2) | async-done | bytes 32800 | tf_op jit(solution)/shard_map/all_to_all | solution.py:152
  133.1 0.1 reshape.261
  133.2 0.1 reshape.253
  133.3 0.1 fusion.34
  133.5 0.2 convolution_convert_fusion.1
  133.7 0.1 reshape.248
  133.8 14.9 %all_to_all.35 = bf16[16,2,2048]{2,1,0:T(2,128)(2,1)} all-to-all(bf16[16,2,2048]{2,1,0:T(2,128)(2,1)S(1)} %reshape.248), channel_id=1, replica_groups=mesh['grp'=16,'dev_0'=4,'dev_1'=8] {'grp'}, dimensions={0} | all-to-all | bytes 262144 | tf_op jit(solution)/shard_map/all_to_all | solution.py:168
  148.8 73.9 %all-gather.2.cloned.1.call-done = bf16[512,2,2048]{2,1,0:T(2,128)(2,1)} async-done(((bf16[16,2,2048]{2,1,0:T(2,128)(2,1)}), bf16[512,2,2048]{2,1,0:T(2,128)(2,1)}) %all-gather.2.cloned.1.call-update) | async-done | bytes 4194320 | tf_op jit(solution)/shard_map/all_gather | solution.py:169
  222.7 7.2 %reshape.249 = bf16[1024,2048]{1,0:T(8,128)(2,1)} reshape(bf16[512,2,2048]{2,1,0:T(2,128)(2,1)} %all-gather.2.cloned.1.call-done) | data formatting | bytes 8388608 | tf_op jit(solution)/shard_map/reshape | solution.py:169
  229.9 4.5 %fusion.8 = f32[1024,256]{1,0:T(8,128)} fusion(bf16[1024,2048]{1,0:T(8,128)(2,1)} %reshape.249, bf16[1,2048,256]{2,1,0:T(8,128)(2,1)S(1)} %copy-done.8), kind=kOutput, calls=%fused_computation.15 | convolution fusion | flops 1073741824 | bytes 6291456 | tf_op jit(solution)/shard_map/dot_general | solution.py:170
  234.4 9.1 %convolution_convert_fusion = bf16[1024,2048]{1,0:T(8,128)(2,1)} fusion(bf16[1024,2048]{1,0:T(8,128)(2,1)} %reshape.249, bf16[1,256,2048]{2,1,0:T(8,128)(2,1)S(1)} %copy-done, bf16[1,2048,256]{2,1,0:T(8,128)(2,1)} %param.30, f32[1024,256]{1,0:T(8,128)} %fusion.8), kind=kOutput, calls=%fused_computation | convolution fusion | flops 2151153664 | bytes 11534336 | tf_op jit(solution)/shard_map/dot_general | solution.py:173
  243.6 0.0 reduce-scatter.5.cloned.1.call-start
  243.6 52.5 %reduce-scatter.3.cloned.1.call-done = bf16[256,2048]{1,0:T(8,128)(2,1)} async-done(((bf16[1024,2048]{1,0:T(8,128)(2,1)}), bf16[256,2048]{1,0:T(8,128)(2,1)}) %reduce-scatter.3.cloned.1.call-update) | async-done | bytes 1048592 | tf_op jit(solution)/shard_map/reduce_scatter | solution.py:49
  296.1 0.1 fusion.41
  296.2 39.4 %reduce-scatter.5.cloned.1.call-done = bf16[32,2048]{1,0:T(8,128)(2,1)} async-done(((bf16[256,2048]{1,0:T(8,128)(2,1)}), bf16[32,2048]{1,0:T(8,128)(2,1)}) %reduce-scatter.5.cloned.1.call-update) | async-done | bytes 131088 | tf_op jit(solution)/shard_map/reduce_scatter | solution.py:49
  335.6 1.6 reshape.250
  337.2 12.5 %all-to-all-start.4 = ((bf16[16,2,2048]{2,1,0:T(2,128)(2,1)}), bf16[16,2,2048]{2,1,0:T(2,128)(2,1)S(1)}, u32[]{:S(2)}, u32[]{:S(2)}) async-start(bf16[16,2,2048]{2,1,0:T(2,128)(2,1)} %reshape.250), calls=%async_computation.6 | async-start | bytes 262144 | tf_op jit(solution)/shard_map/all_to_all | solution.py:174
  349.7 0.3 select_reduce_fusion.2
  350.1 8.8 %all-to-all-done.4 = bf16[16,2,2048]{2,1,0:T(2,128)(2,1)S(1)} async-done(((bf16[16,2,2048]{2,1,0:T(2,128)(2,1)}), bf16[16,2,2048]{2,1,0:T(2,128)(2,1)S(1)}, u32[]{:S(2)}, u32[]{:S(2)}) %all-to-all-start.4) | async-done | bytes 131104 | tf_op jit(solution)/shard_map/all_to_all | solution.py:174
  358.8 0.1 reshape.251
  358.9 0.9 fusion
  (44 shorter events, 0.4 us)
Async XLA Ops:
  6.5 227.9 %copy-start = (bf16[1,256,2048]{2,1,0:T(8,128)(2,1)S(1)}, bf16[1,256,2048]{2,1,0:T(8,128)(2,1)}, u32[]{:S(2)}) copy-start(bf16[1,256,2048]{2,1,0:T(8,128)(2,1)} %param.31) | copy-start | bytes 3145732
  6.5 34.5 %copy-start.5 = (f32[256,2]{0,1:T(2,128)S(1)}, f32[256,2]{0,1:T(2,128)}, u32[]{:S(2)}) copy-start(f32[256,2]{0,1:T(2,128)} %param.18) | copy-start | bytes 6148
  6.5 34.3 %copy-start.2 = (bf16[256,128]{1,0:T(8,128)(2,1)S(1)}, bf16[256,128]{1,0:T(8,128)(2,1)}, u32[]{:S(2)}) copy-start(bf16[256,128]{1,0:T(8,128)(2,1)} %param.21) | copy-start | bytes 196612
  6.5 34.5 %copy-start.10 = (f32[2]{0:T(128)S(1)}, f32[2]{0:T(128)}, u32[]{:S(2)}) copy-start(f32[2]{0:T(128)} %param.22) | copy-start | bytes 28
  6.5 35.3 %copy-start.1 = (bf16[256,128]{1,0:T(8,128)(2,1)S(1)}, bf16[256,128]{1,0:T(8,128)(2,1)}, u32[]{:S(2)}) copy-start(bf16[256,128]{1,0:T(8,128)(2,1)} %param.17) | copy-start | bytes 196612
  6.5 53.7 %copy-start.7 = (f32[128]{0:T(128)S(1)}, f32[128]{0:T(128)}, u32[]{:S(2)}) copy-start(f32[128]{0:T(128)} %param.23) | copy-start | bytes 1540
  41.1 25.2 %copy-start.6 = (s32[8,2]{0,1:T(2,128)S(1)}, s32[8,2]{0,1:T(2,128)}, u32[]{:S(2)}) copy-start(s32[8,2]{0,1:T(2,128)} %param.28) | copy-start | bytes 196
  62.1 71.2 %copy-start.3 = (bf16[8,2048]{1,0:T(8,128)(2,1)S(1)}, bf16[8,2048]{1,0:T(8,128)(2,1)}, u32[]{:S(2)}) copy-start(bf16[8,2048]{1,0:T(8,128)(2,1)} %param.25) | copy-start | bytes 98308
  62.1 71.4 %copy-start.4 = (f32[2048]{0:T(1024)S(1)}, f32[2048]{0:T(1024)}, u32[]{:S(2)}) copy-start(f32[2048]{0:T(1024)} %param.26) | copy-start | bytes 24580
  62.1 53.4 %all-to-all-start.1 = ((bf16[32,256,128]{1,2,0:T(8,128)(2,1)}), bf16[32,256,128]{1,2,0:T(8,128)(2,1)S(1)}, u32[]{:S(2)}, u32[]{:S(2)}) async-start(bf16[32,256,128]{1,2,0:T(8,128)(2,1)} %broadcast_in_dim.81), calls=%async_computation.1 | async-start | bytes 4194304 | tf_op jit(solution)/shard_map/all_to_all | solution.py:26
  117.9 15.2 %all-to-all-start.2 = ((bf16[32,2,256]{2,1,0:T(2,128)(2,1)}), bf16[32,2,256]{2,1,0:T(2,128)(2,1)S(1)}, u32[]{:S(2)}, u32[]{:S(2)}) async-start(bf16[32,2,256]{2,1,0:T(2,128)(2,1)} %reshape.260), calls=%async_computation.2 | async-start | bytes 65536 | tf_op jit(solution)/shard_map/all_to_all | solution.py:152
  124.3 98.4 %all-gather.2.cloned.1.call-start = ((), (), s32[]{:S(2)}) async-start(), calls=%async_computation.7 | async-start | bytes 4325376 | tf_op jit(solution)/shard_map/all_gather | solution.py:169
  148.8 81.2 %copy-start.8 = (bf16[1,2048,256]{2,1,0:T(8,128)(2,1)S(1)}, bf16[1,2048,256]{2,1,0:T(8,128)(2,1)}, u32[]{:S(2)}) copy-start(bf16[1,2048,256]{2,1,0:T(8,128)(2,1)} %param.29) | copy-start | bytes 3145732
  148.8 147.3 %reduce-scatter.3.cloned.1.call-start = ((), (), s32[]{:S(2)}) async-start(), calls=%async_computation.8 | async-start | bytes 5242880 | tf_op jit(solution)/shard_map/reduce_scatter | solution.py:49
  243.5 106.1 %copy-start.9 = (f32[2048,16]{0,1:T(8,128)S(1)}, f32[2048,16]{0,1:T(8,128)}, u32[]{:S(2)}) copy-start(f32[2048,16]{0,1:T(8,128)} %param.27) | copy-start | bytes 393220
  243.6 92.0 %reduce-scatter.5.cloned.1.call-start = ((), (), s32[]{:S(2)}) async-start(), calls=%async_computation.9 | async-start | bytes 1179648 | tf_op jit(solution)/shard_map/reduce_scatter | solution.py:49
  337.2 21.6 %all-to-all-start.4 = ((bf16[16,2,2048]{2,1,0:T(2,128)(2,1)}), bf16[16,2,2048]{2,1,0:T(2,128)(2,1)S(1)}, u32[]{:S(2)}, u32[]{:S(2)}) async-start(bf16[16,2,2048]{2,1,0:T(2,128)(2,1)} %reshape.250), calls=%async_computation.6 | async-start | bytes 262144 | tf_op jit(solution)/shard_map/all_to_all | solution.py:174
Sparse Core Ops, SparseCore 0:
  148.9 73.7 all-gather.1
  243.7 52.3 reduce-scatter.2
  299.1 36.3 reduce-scatter.4
where the time goes:
time: 367 us; the launch traced here: 366 us
  waiting for transfers between devices  232 us (63%)
  blocking collectives  59.1 us (16%)
  starting transfers between devices  23.1 us (6%)
  matrix products  20.1 us (5%)
  local copies, waits for them, and re-layouts  15 us (4%)
  between operations  13.4 us (4%)
  other arithmetic  3.74 us (1%)
    reduce_scatter x2, waiting for transfers between devices, sum_by_axis(): total = lax.psum_scatter(total, axis, scatter_dimension=0, tiled=True)  91.8 us
    all_gather x1, waiting for transfers between devices, shards(): lax.all_gather(arrived, DEV, axis=0, tiled=True).reshape(-1, model_dim)  73.9 us
    all_to_all x1, waiting for transfers between devices, sent_to_all(): lax.all_to_all(jnp.broadcast_to(shard[None], (peers, *shard.shape)), axis...  48.6 us
    all_gather x1, blocking collectives, side_by_side(): lax.all_gather(both, axis, axis=dim, tiled=True)  26 us
    all_to_all x1, blocking collectives, sent_to_all(): lax.all_to_all(jnp.broadcast_to(shard[None], (peers, *shard.shape)), axis...  18.2 us
    all_to_all x1, blocking collectives, shards(): lax.all_to_all(outgoing, 'grp', split_axis=0, concat_axis=0, tiled=True)  14.9 us
    all_to_all x1, starting transfers between devices, shards(): lax.all_to_all(summed.astype(jnp.bfloat16).reshape(experts, slot_cap, mod...  12.5 us
    dot_general x1, matrix products, shards(): jnp.dot(hidden, down_weight[0], preferred_element_type=jnp.float32)  9.1 us
  transfers between devices with their start and end apart: 6, of which 6 were waited for; matrix products, arithmetic and copies ran while one was open for 0% of the time, Pallas kernels for 0%

commit v1 on v0

--- a/solution.py
+++ b/solution.py
@@ -149,7 +149,10 @@
     projected = jnp.dot(
         collect(mixed_rows, DEV, 1), out_proj, preferred_element_type=jnp.float32
     ).astype(jnp.bfloat16)
-    mamba_out = lax.all_to_all(projected, DEV, split_axis=0, concat_axis=1, tiled=True)
+    mamba_out = jnp.concatenate(
+        lax.all_to_all(jnp.stack(jnp.split(projected, lax.axis_size(DEV), axis=0)), DEV, 0, 0),
+        axis=1,
+    )
     hidden_res = (residual.astype(jnp.float32) + mamba_out.astype(jnp.float32)).astype(jnp.bfloat16)
     hidden_float = hidden_res.astype(jnp.float32)
     normed = rms_scale(hidden_float, ffn_gain).astype(jnp.bfloat16)

time: 367 us -> 370 us (level)
  no operation moved by 1% of the time
where the time goes in v1:
time: 370 us; the launch traced here: 369 us
  waiting for transfers between devices  232 us (63%)
  blocking collectives  59.1 us (16%)
  starting transfers between devices  23.3 us (6%)
  matrix products  20.1 us (5%)
  local copies, waits for them, and re-layouts  18.1 us (5%)
  between operations  13.5 us (4%)
  other arithmetic  3.74 us (1%)
    reduce_scatter x2, waiting for transfers between devices, sum_by_axis(): total = lax.psum_scatter(total, axis, scatter_dimension=0, tiled=True)  91.9 us
    all_gather x1, waiting for transfers between devices, shards(): lax.all_gather(arrived, DEV, axis=0, tiled=True).reshape(-1, model_dim)  73.7 us
    all_to_all x1, waiting for transfers between devices, sent_to_all(): lax.all_to_all(jnp.broadcast_to(shard[None], (peers, *shard.shape)), axis...  48.6 us
    all_gather x1, blocking collectives, side_by_side(): lax.all_gather(both, axis, axis=dim, tiled=True)  26 us
    all_to_all x1, blocking collectives, sent_to_all(): lax.all_to_all(jnp.broadcast_to(shard[None], (peers, *shard.shape)), axis...  18.2 us
    all_to_all x1, blocking collectives, shards(): lax.all_to_all(outgoing, 'grp', split_axis=0, concat_axis=0, tiled=True)  14.9 us
    all_to_all x1, starting transfers between devices, shards(): lax.all_to_all(summed.astype(jnp.bfloat16).reshape(experts, slot_cap, mod...  12.4 us
    dot_general x1, matrix products, shards(): jnp.dot(hidden, down_weight[0], preferred_element_type=jnp.float32)  9.1 us
  transfers between devices with their start and end apart: 6, of which 6 were waited for; matrix products, arithmetic and copies ran while one was open for 0% of the time, Pallas kernels for 0%

profile of v1, /device:TPU:1, one launch (start us, length us, event | category | flops | bytes accessed | tf_op | source)
XLA Modules:
  0.0 369.5 jit_solution(9041834502989573428)
XLA Ops:
  6.6 0.9 negate_bitcast_fusion
  7.4 0.6 reduce-window.6
  8.1 0.2 slice_reduce_fusion
  8.2 0.2 reduce-window.9
  8.5 0.2 slice_reduce_fusion.1
  8.7 0.9 copy.165
  9.7 0.8 fusion.55
  10.4 1.0 convolution_convert_fusion.2
  11.5 0.1 pad_maximum_fusion
  11.6 26.0 %all_gather.6 = bf16[16,2,8193]{2,1,0:T(2,128)(2,1)S(1)} all-gather(bf16[1,2,8193]{2,1,0:T(2,128)(2,1)S(1)} %pad_maximum_fusion), channel_id=1, replica_groups=mesh['grp'=16,'dev_0'=4,'dev_1'=8] {'grp'}, dimensions={0}, use_global_device_ids=true | all-gather | bytes 557124 | tf_op jit(solution)/shard_map/all_gather | solution.py:16
  37.6 0.7 slice.40
  38.3 0.1 copy.213
  38.4 0.1 copy.168
  38.5 0.1 select_reduce_fusion.1
  38.8 0.4 reshape.244
  39.2 1.1 fusion.56
  40.3 0.6 fusion.15
  40.8 0.2 fusion.4
  41.1 0.6 fusion.3
  41.7 0.1 copy.170
  41.8 0.1 multiply_reduce_fusion
  42.0 18.2 %all_to_all.26 = f32[32,1,256]{2,1,0:T(1,128)S(1)} all-to-all(f32[32,1,256]{2,1,0:T(1,128)S(1)} %broadcast_in_dim.80), channel_id=1, replica_groups=mesh['grp'=16,'dev_0'=4,'dev_1'=8] {'dev_0','dev_1'}, dimensions={0} | all-to-all | bytes 65536 | tf_op jit(solution)/shard_map/all_to_all | solution.py:26
  60.3 0.1 multiply_convert_fusion
  60.4 0.1 copy.172
  60.5 1.6 broadcast_in_dim.81
  62.1 4.1 %all-to-all-start.1 = ((bf16[32,256,128]{1,2,0:T(8,128)(2,1)}), bf16[32,256,128]{1,2,0:T(8,128)(2,1)S(1)}, u32[]{:S(2)}, u32[]{:S(2)}) async-start(bf16[32,256,128]{1,2,0:T(8,128)(2,1)} %broadcast_in_dim.81), calls=%async_computation.1 | async-start | bytes 4194304 | tf_op jit(solution)/shard_map/all_to_all | solution.py:26
  66.5 0.2 select_reduce_fusion
  66.8 0.1 copy.208
  66.9 48.6 %all-to-all-done.1 = bf16[32,256,128]{1,2,0:T(8,128)(2,1)S(1)} async-done(((bf16[32,256,128]{1,2,0:T(8,128)(2,1)}), bf16[32,256,128]{1,2,0:T(8,128)(2,1)S(1)}, u32[]{:S(2)}, u32[]{:S(2)}) %all-to-all-start.1) | async-done | bytes 2097184 | tf_op jit(solution)/shard_map/all_to_all | solution.py:26
  115.5 1.5 convolution_convert_fusion.3
  117.0 0.1 slice_bitcast_fusion.19
  117.1 0.2 slice_bitcast_fusion
  117.5 0.1 copy.175
  117.5 0.1 copy.176
  117.6 0.1 copy.177
  117.8 0.1 copy.179
  117.9 0.1 copy.180
  118.0 0.1 copy.181
  118.1 0.1 copy.182
  118.2 0.1 copy.184
  118.3 0.1 copy.185
  118.4 0.1 copy.186
  118.5 0.1 copy.187
  120.3 0.7 reshape.259
  121.1 6.4 %all-to-all-start.2 = ((bf16[32,2,256]{2,1,0:T(2,128)(2,1)}), bf16[32,2,256]{2,1,0:T(2,128)(2,1)S(1)}, u32[]{:S(2)}, u32[]{:S(2)}) async-start(bf16[32,2,256]{2,1,0:T(2,128)(2,1)} %reshape.259), calls=%async_computation.2 | async-start | bytes 65536 | tf_op jit(solution)/shard_map/all_to_all | solution.py:153
  127.6 8.6 %all-to-all-done.2 = bf16[32,2,256]{2,1,0:T(2,128)(2,1)S(1)} async-done(((bf16[32,2,256]{2,1,0:T(2,128)(2,1)}), bf16[32,2,256]{2,1,0:T(2,128)(2,1)S(1)}, u32[]{:S(2)}, u32[]{:S(2)}) %all-to-all-start.2) | async-done | bytes 32800 | tf_op jit(solution)/shard_map/all_to_all | solution.py:153
  136.2 0.1 reshape.260
  136.4 0.1 reshape.252
  136.5 0.1 fusion.34
  136.7 0.2 convolution_convert_fusion.1
  136.9 0.1 reshape.247
  137.0 14.9 %all_to_all.27 = bf16[16,2,2048]{2,1,0:T(2,128)(2,1)} all-to-all(bf16[16,2,2048]{2,1,0:T(2,128)(2,1)S(1)} %reshape.247), channel_id=1, replica_groups=mesh['grp'=16,'dev_0'=4,'dev_1'=8] {'grp'}, dimensions={0} | all-to-all | bytes 262144 | tf_op jit(solution)/shard_map/all_to_all | solution.py:171
  152.0 0.2 reduce-scatter.3.cloned.1.call-start
  152.2 73.7 %all-gather.2.cloned.1.call-done = bf16[512,2,2048]{2,1,0:T(2,128)(2,1)} async-done(((bf16[16,2,2048]{2,1,0:T(2,128)(2,1)}), bf16[512,2,2048]{2,1,0:T(2,128)(2,1)}) %all-gather.2.cloned.1.call-update) | async-done | bytes 4194320 | tf_op jit(solution)/shard_map/all_gather | solution.py:172
  225.9 7.2 %reshape.248 = bf16[1024,2048]{1,0:T(8,128)(2,1)} reshape(bf16[512,2,2048]{2,1,0:T(2,128)(2,1)} %all-gather.2.cloned.1.call-done) | data formatting | bytes 8388608 | tf_op jit(solution)/shard_map/reshape | solution.py:172
  233.1 4.5 %fusion.8 = f32[1024,256]{1,0:T(8,128)} fusion(bf16[1024,2048]{1,0:T(8,128)(2,1)} %reshape.248, bf16[1,2048,256]{2,1,0:T(8,128)(2,1)S(1)} %copy-done.8), kind=kOutput, calls=%fused_computation.15 | convolution fusion | flops 1073741824 | bytes 6291456 | tf_op jit(solution)/shard_map/dot_general | solution.py:173
  237.6 9.1 %convolution_convert_fusion = bf16[1024,2048]{1,0:T(8,128)(2,1)} fusion(bf16[1024,2048]{1,0:T(8,128)(2,1)} %reshape.248, bf16[1,256,2048]{2,1,0:T(8,128)(2,1)S(1)} %copy-done, bf16[1,2048,256]{2,1,0:T(8,128)(2,1)} %param.30, f32[1024,256]{1,0:T(8,128)} %fusion.8), kind=kOutput, calls=%fused_computation | convolution fusion | flops 2151153664 | bytes 11534336 | tf_op jit(solution)/shard_map/dot_general | solution.py:176
  246.8 52.5 %reduce-scatter.3.cloned.1.call-done = bf16[256,2048]{1,0:T(8,128)(2,1)} async-done(((bf16[1024,2048]{1,0:T(8,128)(2,1)}), bf16[256,2048]{1,0:T(8,128)(2,1)}) %reduce-scatter.3.cloned.1.call-update) | async-done | bytes 1048592 | tf_op jit(solution)/shard_map/reduce_scatter | solution.py:49
  299.4 39.4 %reduce-scatter.5.cloned.1.call-done = bf16[32,2048]{1,0:T(8,128)(2,1)} async-done(((bf16[256,2048]{1,0:T(8,128)(2,1)}), bf16[32,2048]{1,0:T(8,128)(2,1)}) %reduce-scatter.5.cloned.1.call-update) | async-done | bytes 131088 | tf_op jit(solution)/shard_map/reduce_scatter | solution.py:49
  338.8 1.6 reshape.249
  340.4 12.4 %all-to-all-start.4 = ((bf16[16,2,2048]{2,1,0:T(2,128)(2,1)}), bf16[16,2,2048]{2,1,0:T(2,128)(2,1)S(1)}, u32[]{:S(2)}, u32[]{:S(2)}) async-start(bf16[16,2,2048]{2,1,0:T(2,128)(2,1)} %reshape.249), calls=%async_computation.6 | async-start | bytes 262144 | tf_op jit(solution)/shard_map/all_to_all | solution.py:177
  352.9 0.3 select_reduce_fusion.2
  353.2 8.8 %all-to-all-done.4 = bf16[16,2,2048]{2,1,0:T(2,128)(2,1)S(1)} async-done(((bf16[16,2,2048]{2,1,0:T(2,128)(2,1)}), bf16[16,2,2048]{2,1,0:T(2,128)(2,1)S(1)}, u32[]{:S(2)}, u32[]{:S(2)}) %all-to-all-start.4) | async-done | bytes 131104 | tf_op jit(solution)/shard_map/all_to_all | solution.py:177
  362.1 0.9 fusion
  (109 shorter events, 3.3 us)
Async XLA Ops:
  6.5 231.1 %copy-start = (bf16[1,256,2048]{2,1,0:T(8,128)(2,1)S(1)}, bf16[1,256,2048]{2,1,0:T(8,128)(2,1)}, u32[]{:S(2)}) copy-start(bf16[1,256,2048]{2,1,0:T(8,128)(2,1)} %param.31) | copy-start | bytes 3145732
  6.5 34.5 %copy-start.5 = (f32[256,2]{0,1:T(2,128)S(1)}, f32[256,2]{0,1:T(2,128)}, u32[]{:S(2)}) copy-start(f32[256,2]{0,1:T(2,128)} %param.18) | copy-start | bytes 6148
  6.5 34.3 %copy-start.2 = (bf16[256,128]{1,0:T(8,128)(2,1)S(1)}, bf16[256,128]{1,0:T(8,128)(2,1)}, u32[]{:S(2)}) copy-start(bf16[256,128]{1,0:T(8,128)(2,1)} %param.21) | copy-start | bytes 196612
  6.5 34.5 %copy-start.10 = (f32[2]{0:T(128)S(1)}, f32[2]{0:T(128)}, u32[]{:S(2)}) copy-start(f32[2]{0:T(128)} %param.22) | copy-start | bytes 28
  6.5 35.3 %copy-start.1 = (bf16[256,128]{1,0:T(8,128)(2,1)S(1)}, bf16[256,128]{1,0:T(8,128)(2,1)}, u32[]{:S(2)}) copy-start(bf16[256,128]{1,0:T(8,128)(2,1)} %param.17) | copy-start | bytes 196612
  6.5 53.7 %copy-start.7 = (f32[128]{0:T(128)S(1)}, f32[128]{0:T(128)}, u32[]{:S(2)}) copy-start(f32[128]{0:T(128)} %param.23) | copy-start | bytes 1540
  41.1 25.2 %copy-start.6 = (s32[8,2]{0,1:T(2,128)S(1)}, s32[8,2]{0,1:T(2,128)}, u32[]{:S(2)}) copy-start(s32[8,2]{0,1:T(2,128)} %param.28) | copy-start | bytes 196
  62.1 74.4 %copy-start.3 = (bf16[8,2048]{1,0:T(8,128)(2,1)S(1)}, bf16[8,2048]{1,0:T(8,128)(2,1)}, u32[]{:S(2)}) copy-start(bf16[8,2048]{1,0:T(8,128)(2,1)} %param.25) | copy-start | bytes 98308
  62.1 74.6 %copy-start.4 = (f32[2048]{0:T(1024)S(1)}, f32[2048]{0:T(1024)}, u32[]{:S(2)}) copy-start(f32[2048]{0:T(1024)} %param.26) | copy-start | bytes 24580
  62.1 53.4 %all-to-all-start.1 = ((bf16[32,256,128]{1,2,0:T(8,128)(2,1)}), bf16[32,256,128]{1,2,0:T(8,128)(2,1)S(1)}, u32[]{:S(2)}, u32[]{:S(2)}) async-start(bf16[32,256,128]{1,2,0:T(8,128)(2,1)} %broadcast_in_dim.81), calls=%async_computation.1 | async-start | bytes 4194304 | tf_op jit(solution)/shard_map/all_to_all | solution.py:26
  121.1 15.2 %all-to-all-start.2 = ((bf16[32,2,256]{2,1,0:T(2,128)(2,1)}), bf16[32,2,256]{2,1,0:T(2,128)(2,1)S(1)}, u32[]{:S(2)}, u32[]{:S(2)}) async-start(bf16[32,2,256]{2,1,0:T(2,128)(2,1)} %reshape.259), calls=%async_computation.2 | async-start | bytes 65536 | tf_op jit(solution)/shard_map/all_to_all | solution.py:153
  127.5 98.4 %all-gather.2.cloned.1.call-start = ((), (), s32[]{:S(2)}) async-start(), calls=%async_computation.7 | async-start | bytes 4325376 | tf_op jit(solution)/shard_map/all_gather | solution.py:172
  152.0 81.2 %copy-start.8 = (bf16[1,2048,256]{2,1,0:T(8,128)(2,1)S(1)}, bf16[1,2048,256]{2,1,0:T(8,128)(2,1)}, u32[]{:S(2)}) copy-start(bf16[1,2048,256]{2,1,0:T(8,128)(2,1)} %param.29) | copy-start | bytes 3145732
  152.0 147.3 %reduce-scatter.3.cloned.1.call-start = ((), (), s32[]{:S(2)}) async-start(), calls=%async_computation.8 | async-start | bytes 5242880 | tf_op jit(solution)/shard_map/reduce_scatter | solution.py:49
  246.7 106.1 %copy-start.9 = (f32[2048,16]{0,1:T(8,128)S(1)}, f32[2048,16]{0,1:T(8,128)}, u32[]{:S(2)}) copy-start(f32[2048,16]{0,1:T(8,128)} %param.27) | copy-start | bytes 393220
  246.8 92.0 %reduce-scatter.5.cloned.1.call-start = ((), (), s32[]{:S(2)}) async-start(), calls=%async_computation.9 | async-start | bytes 1179648 | tf_op jit(solution)/shard_map/reduce_scatter | solution.py:49
  340.4 21.6 %all-to-all-start.4 = ((bf16[16,2,2048]{2,1,0:T(2,128)(2,1)}), bf16[16,2,2048]{2,1,0:T(2,128)(2,1)S(1)}, u32[]{:S(2)}, u32[]{:S(2)}) async-start(bf16[16,2,2048]{2,1,0:T(2,128)(2,1)} %reshape.249), calls=%async_computation.6 | async-start | bytes 262144 | tf_op jit(solution)/shard_map/all_to_all | solution.py:177
Sparse Core Ops, SparseCore 0:
  152.1 73.7 all-gather.1
  246.9 52.3 reduce-scatter.2
  302.4 36.3 reduce-scatter.4
